TPU v7x, 256 devices: a whole 4x4x8 slice. The times are simulated.
256 devices in a mesh: dom: 64 (over y, z, core), rep: 4 (over x).
Axes of the slice: x: 4, y: 4, z: 8, core: 2. Of those that a mesh axis runs over, the one named last changes fastest.
Arguments:
- x_loader: bfloat16 [131072, 512], P(('dom', 'rep')), may hold values from -6 to 6
- owner_index: int32 [131072], P(('dom', 'rep')), may hold values from 0 to 131071, as said below
- tile_vals: bfloat16 [1024, 12, 128, 128], P(('dom', 'rep')), as said below
- tile_cols: int32 [1024, 12], P(('dom', 'rep')), may hold values from 0 to 1023, as said below
- tile_live: int32 [1024, 12], P(('dom', 'rep')), may hold values from 0 to 1, as said below
- w_self: bfloat16 [512, 512], replicated, may hold values from -0.25 to 0.25
- w_neigh: bfloat16 [512, 512], replicated, may hold values from -3 to 3
- bias: float32 [512], replicated, may hold values from -3 to 3
- cotangent: bfloat16 [131072, 512], P(('dom', 'rep')), may hold values from -6 to 6
Outputs:
- layer_out: bfloat16 [131072, 512], P(('dom', 'rep'))
- grad_features: bfloat16 [131072, 512], P(('dom', 'rep'))
- grad_self: float32 [512, 512], replicated
- grad_neigh: float32 [512, 512], replicated
- grad_bias: float32 [512], replicated
Inputs may be any that keep to these rules, and one draw needn't show every extreme that they name: `owner_index`: A permutation of the 131072 rows. Loader rows are in blocks of 512 in the order of the devices (dom slowest); owner rows likewise. The 512 rows of each loader block with rep index r go to owner blocks of rep index r, 8 rows to each of the 64 partitions. `tile_cols`: partition p holds row tiles p * 16 to (p + 1) * 16 - 1. A column tile of a row tile of partition p lies in partition p or within 4 tiles beyond its edges. W is symmetric: every live slot (t, c) with tiles B is matched by a live slot (c, t) with tiles B^T, a slot with c = t holding a symmetric tile. `tile_live`: live slots are symmetric as stated for tile_cols. `tile_vals`: nonnegative edge weights.
All inputs are finite; a program needn't handle non-finite values.
Results may differ from a plain program's by a relative error of at most 0.0075.
Values may be sent and summed in bfloat16 or wider, within the bound.
No kernel may reach another device: no remote copies, remote signals or barrier semaphores. Data moves between devices by JAX's collectives and lax.ppermute only.
A program may use at most 64 MiB of HBM per device.

v0:
```python
import jax
import jax.numpy as jnp
from jax import lax
from jax.sharding import PartitionSpec as P

HALO_T = 4


def shifted(value, axis, steps):
    count = lax.axis_size(axis)
    first, last = (max(0, -steps), min(count, count - steps))
    return lax.ppermute(value, axis, [(source, source + steps) for source in range(first, last)])


def with_halo(block, sides, width):
    for axis, dim in sides:
        count = lax.axis_size(axis)
        forward = [(i, i + 1) for i in range(count - 1)]
        backward = [(target, source) for source, target in forward]
        low = lax.ppermute(
            lax.slice_in_dim(block, block.shape[dim] - width, None, axis=dim), axis, forward
        )
        high = lax.ppermute(lax.slice_in_dim(block, 0, width, axis=dim), axis, backward)
        block = jnp.concatenate([low, block, high], axis=dim)
    return block


def contract_rows(left, right):
    return lax.dot_general(
        left, right, (((0,), (0,)), ((), ())), preferred_element_type=jnp.float32
    )


def contract_cols(left, right):
    return lax.dot_general(
        left, right, (((1,), (1,)), ((), ())), preferred_element_type=jnp.float32
    )


def pass_rim(values, offset):
    return shifted(values.astype(jnp.bfloat16), "dom", offset).astype(values.dtype)


def shards(
    x_loader, owner_index, tile_vals, tile_cols, tile_live, w_self, w_neigh, bias, cotangent
):
    rows, width = x_loader.shape
    reps = lax.axis_size("rep")
    dom_place = lax.axis_index("dom")
    part_rows = rows * reps
    part_tiles = part_rows // 128
    row_tiles = rows // 128
    rim_rows = HALO_T * 128
    dest = owner_index // part_rows
    order = jnp.argsort(dest, stable=True)
    moved, slot = (
        lax.all_to_all(x_loader[order], "dom", split_axis=0, concat_axis=0, tiled=True),
        lax.all_to_all((owner_index % rows)[order], "dom", split_axis=0, concat_axis=0, tiled=True),
    )
    features = jnp.zeros((rows, width), jnp.bfloat16).at[slot].set(moved)
    first_tile = dom_place * part_tiles - HALO_T
    local_cols = tile_cols - first_tile
    masked = tile_vals * tile_live.astype(jnp.bfloat16)[:, :, None, None]
    degree = 1.0 + jnp.sum(masked, axis=(1, 3), dtype=jnp.float32)
    whole = lax.all_gather(features, "rep", axis=0, tiled=True)
    extended = with_halo(whole, (("dom", 0),), rim_rows)
    picked = extended.reshape(-1, 128, width)[local_cols]
    summed = jnp.einsum("tkab,tkbf->taf", masked, picked, preferred_element_type=jnp.float32)
    agg = (summed / degree[:, :, None]).reshape(rows, width).astype(jnp.bfloat16)
    pre = (
        jnp.dot(features, w_self, preferred_element_type=jnp.float32)
        + jnp.dot(agg, w_neigh, preferred_element_type=jnp.float32)
        + bias
    )
    layer_out = jnp.where(pre > 0, pre, jnp.expm1(jnp.minimum(pre, 0.0))).astype(jnp.bfloat16)
    slope = jnp.where(pre > 0, 1.0, jnp.exp(jnp.minimum(pre, 0.0)))
    dz = (cotangent.astype(jnp.float32) * slope).astype(jnp.bfloat16)
    grad_self, grad_neigh, grad_bias = lax.psum(
        (
            contract_rows(features, dz),
            contract_rows(agg, dz),
            jnp.sum(dz, axis=0, dtype=jnp.float32),
        ),
        ("dom", "rep"),
    )
    scaled = (contract_cols(dz, w_neigh) / degree.reshape(rows, 1)).astype(jnp.bfloat16)
    terms = jnp.einsum(
        "tkab,taf->tkbf",
        masked,
        scaled.reshape(row_tiles, 128, width),
        preferred_element_type=jnp.float32,
    )
    span_tiles = part_tiles + 2 * HALO_T
    selector = (
        local_cols.reshape(-1)[None, :] == jnp.arange(span_tiles, dtype=jnp.int32)[:, None]
    ).astype(jnp.float32)
    buffer = jnp.einsum(
        "en,nbf->ebf", selector, terms.reshape(-1, 128, width), precision=lax.Precision.HIGHEST
    )
    buffer = buffer.reshape(span_tiles * 128, width)
    lower = buffer[:rim_rows]
    upper = buffer[rim_rows + part_rows :]
    core = buffer[rim_rows : rim_rows + part_rows]
    core = core.at[:rim_rows].add(pass_rim(upper, 1))
    core = core.at[part_rows - rim_rows :].add(pass_rim(lower, -1))
    back = lax.psum_scatter(core, "rep", scatter_dimension=0, tiled=True)
    grad_features = (contract_cols(dz, w_self) + back).astype(jnp.bfloat16)
    return (layer_out, grad_features, grad_self, grad_neigh, grad_bias)


def solution(mesh):
    return jax.shard_map(
        shards,
        mesh=mesh,
        in_specs=(
            P(("dom", "rep"), None),
            P(("dom", "rep")),
            P(("dom", "rep"), None, None, None),
            P(("dom", "rep"), None),
            P(("dom", "rep"), None),
            P(),
            P(),
            P(),
            P(("dom", "rep"), None),
        ),
        out_specs=(P(("dom", "rep"), None), P(("dom", "rep"), None), P(), P(), P()),
        check_vma=False,
    )
```

profile of v0, /device:TPU:2, one launch (start us, length us, event | category | flops | bytes accessed | tf_op | source)
XLA Modules:
  0.0 486.7 jit_solution(7837561082085686232)
XLA Ops:
  8.0 3.8 sort.17
  11.8 3.5 gather_fusion
  16.0 12.1 %all-to-all-start = ((s32[64,8,1]{1,2,0:T(1,128)}), s32[64,8,1]{1,2,0:T(1,128)S(1)}, u32[]{:S(2)}, u32[]{:S(2)}) async-start(s32[64,8,1]{1,2,0:T(1,128)} %bitcast), calls=%async_computation | async-start | bytes 65536 | tf_op jit(solution)/shard_map/all_to_all | solution.py:58
  28.1 2.6 gather_fusion.1
  30.7 6.8 %all-to-all-done = s32[64,8,1]{1,2,0:T(1,128)S(1)} async-done(((s32[64,8,1]{1,2,0:T(1,128)}), s32[64,8,1]{1,2,0:T(1,128)S(1)}, u32[]{:S(2)}, u32[]{:S(2)}) %all-to-all-start) | async-done | bytes 2080 | tf_op jit(solution)/shard_map/all_to_all | solution.py:58
  37.5 4.6 all-to-all-start.1
  43.6 15.8 %all-to-all-done.1 = bf16[64,8,512]{2,1,0:T(8,128)(2,1)S(1)} async-done(((bf16[64,8,512]{2,1,0:T(8,128)(2,1)}), bf16[64,8,512]{2,1,0:T(8,128)(2,1)S(1)}, u32[]{:S(2)}, u32[]{:S(2)}) %all-to-all-start.1) | async-done | bytes 524320 | tf_op jit(solution)/shard_map/all_to_all | solution.py:57
  59.4 3.2 scatter_custom_fusion
  63.2 29.2 %all-gather.2.cloned.1.call-done = bf16[2048,512]{1,0:T(8,128)(2,1)} async-done(((bf16[512,512]{1,0:T(8,128)(2,1)}), bf16[2048,512]{1,0:T(8,128)(2,1)}) %all-gather.2.cloned.1.call-update) | async-done | bytes 2097168 | tf_op jit(solution)/shard_map/all_gather | solution.py:65
  92.4 2.2 fusion.26
  94.6 2.5 collective-permute-start
  101.9 3.1 pad_maximum_fusion
  105.0 6.8 %gather_fusion.2 = bf16[48,128,512]{2,1,0:T(8,128)(2,1)} fusion(bf16[24,128,512]{2,1,0:T(8,128)(2,1)} %bitcast.50, s32[1024]{0:T(1024)S(1)} %pad_clamp_fusion), kind=kCustom, calls=%fused_computation.2 | custom fusion | bytes 12583104 | tf_op jit(solution)/shard_map/gather | solution.py:67
  111.9 4.0 fusion.5
  118.1 1.9 fusion.6
  120.1 12.3 %fusion.27 = (bf16[24,128,512]{2,0,1:T(8,128)(2,1)S(1)}, f32[24,128,512]{2,0,1:T(8,128)S(1)}) fusion(f32[48,128,512]{2,1,0:T(8,128)S(1)} %bitcast.49, s32[48]{0:T(128)S(1)} %eq.17), kind=kOutput, calls=%fused_computation.56 | convolution fusion | flops 907543680 | bytes 22020288 | tf_op jit(solution)/shard_map/en,nbf->ebf/dot_general | solution.py:97
  132.9 9.1 %collective-permute-start.2 = (bf16[512,512]{1,0:T(8,128)(2,1)S(1)}, bf16[512,512]{1,0:T(8,128)(2,1)S(1)}, u32[]{:S(2)}, u32[]{:S(2)}) collective-permute-start(bf16[512,512]{1,0:T(8,128)(2,1)S(1)} %bitcast.54), channel_id=1, source_target_pairs={{0,4},{4,8},{8,12},{12,16},{16,20},{20,24},{24,28},{28,32},{32,36}... | collective-permute-start | bytes 1572872 | tf_op jit(solution)/shard_map/ppermute | solution.py:12
  144.7 4.4 copy.29
  150.6 2.4 fusion.12
  156.0 83.0 %psum.23 = f32[512]{0:T(512)} all-reduce(f32[512]{0:T(512)S(1)} %get-tuple-element.33), channel_id=1, replica_groups=mesh['dom'=64,'rep'=4] {'dom','rep'}, use_global_device_ids=true, to_apply=%region_7.8 | all-reduce | flops 512 | bytes 4096 | tf_op jit(solution)/shard_map/psum | solution.py:78
  239.5 2.2 add_convert_fusion
  241.7 234.0 %all-reduce.3.cloned.1.call-done = (f32[512,512]{1,0:T(8,128)}, f32[512,512]{1,0:T(8,128)}) async-done(((f32[512,512]{1,0:T(8,128)}, f32[512,512]{1,0:T(8,128)}), (f32[512,512]{1,0:T(8,128)}, f32[512,512]{1,0:T(8,128)})) %all-reduce.3.cloned.1.call-update) | async-done | bytes 2097168 | tf_op jit(solution)/shard_map/psum | solution.py:78
  475.6 2.3 copy.44
  477.9 2.3 copy.45
  (68 shorter events, 18.5 us)
Async XLA Ops:
  7.2 108.7 %copy-start = (bf16[512,512]{1,0:T(8,128)(2,1)S(1)}, bf16[512,512]{1,0:T(8,128)(2,1)}, u32[]{:S(2)}) copy-start(bf16[512,512]{1,0:T(8,128)(2,1)} %param.19) | copy-start | bytes 1572868
  7.2 20.9 %copy-start.1 = (bf16[512,512]{1,0:T(8,128)(2,1)S(1)}, bf16[512,512]{1,0:T(8,128)(2,1)}, u32[]{:S(2)}) copy-start(bf16[512,512]{1,0:T(8,128)(2,1)} %param.13) | copy-start | bytes 1572868
  15.3 47.4 %copy-start.10 = (s32[4,12]{1,0:T(4,128)S(1)}, s32[4,12]{1,0:T(4,128)}, u32[]{:S(2)}) copy-start(s32[4,12]{1,0:T(4,128)} %param.16) | copy-start | bytes 580
  15.3 47.5 %copy-start.9 = (s32[4,12]{1,0:T(4,128)S(1)}, s32[4,12]{1,0:T(4,128)}, u32[]{:S(2)}) copy-start(s32[4,12]{1,0:T(4,128)} %param.17) | copy-start | bytes 580
  15.3 47.5 %copy-start.3 = (bf16[4,12,128,128]{3,2,1,0:T(8,128)(2,1)S(1)}, bf16[4,12,128,128]{3,2,1,0:T(8,128)(2,1)}, u32[]{:S(2)}) copy-start(bf16[4,12,128,128]{3,2,1,0:T(8,128)(2,1)} %param.15) | copy-start | bytes 4718596
  16.0 21.5 %all-to-all-start = ((s32[64,8,1]{1,2,0:T(1,128)}), s32[64,8,1]{1,2,0:T(1,128)S(1)}, u32[]{:S(2)}, u32[]{:S(2)}) async-start(s32[64,8,1]{1,2,0:T(1,128)} %bitcast), calls=%async_computation | async-start | bytes 65536 | tf_op jit(solution)/shard_map/all_to_all | solution.py:58
  30.7 67.8 %copy-start.4 = (bf16[512,512]{1,0:T(8,128)(2,1)S(1)}, bf16[512,512]{1,0:T(8,128)(2,1)}, u32[]{:S(2)}) copy-start(bf16[512,512]{1,0:T(8,128)(2,1)} %param.18) | copy-start | bytes 1572868
  37.5 21.8 %all-to-all-start.1 = ((bf16[64,8,512]{2,1,0:T(8,128)(2,1)}), bf16[64,8,512]{2,1,0:T(8,128)(2,1)S(1)}, u32[]{:S(2)}, u32[]{:S(2)}) async-start(bf16[64,8,512]{2,1,0:T(8,128)(2,1)} %bitcast.2), calls=%async_computation.1 | async-start | bytes 1048576 | tf_op jit(solution)/shard_map/all_to_all | solution.py:57
  42.2 50.2 %all-gather.2.cloned.1.call-start = ((), (), s32[]{:S(2)}) async-start(), calls=%async_computation.3 | async-start | bytes 2621440 | tf_op jit(solution)/shard_map/all_gather | solution.py:65
  62.5 36.0 %copy-start.2 = (bf16[512,512]{1,0:T(8,128)(2,1)S(1)}, bf16[512,512]{1,0:T(8,128)(2,1)}, u32[]{:S(2)}) copy-start(bf16[512,512]{1,0:T(8,128)(2,1)} %scatter_custom_fusion) | copy-start | bytes 1572868
  62.6 176.9 %reduce-scatter.2.cloned.1.call-start = ((), (), s32[]{:S(2)}) async-start(), calls=%async_computation.4 | async-start | bytes 5242880 | tf_op jit(solution)/shard_map/reduce_scatter | solution.py:106
  94.6 5.3 %collective-permute-start = (bf16[512,512]{1,0:T(8,128)(2,1)}, bf16[512,512]{1,0:T(8,128)(2,1)}, u32[]{:S(2)}, u32[]{:S(2)}) collective-permute-start(bf16[512,512]{1,0:T(8,128)(2,1)} %get-tuple-element.39), channel_id=1, source_target_pairs={{0,4},{4,8},{8,12},{12,16},{16,20},{20,24},{24,28},{28,32},{32,36}... | collective-permute-start | bytes 1572872 | tf_op jit(solution)/shard_map/ppermute | solution.py:20
  97.2 4.7 collective-permute-start.1
  111.8 4.1 copy-start.6
  111.9 4.1 copy-start.11
  111.9 4.1 copy-start.12
  115.9 2.3 copy-start.7
  132.9 16.5 %collective-permute-start.2 = (bf16[512,512]{1,0:T(8,128)(2,1)S(1)}, bf16[512,512]{1,0:T(8,128)(2,1)S(1)}, u32[]{:S(2)}, u32[]{:S(2)}) collective-permute-start(bf16[512,512]{1,0:T(8,128)(2,1)S(1)} %bitcast.54), channel_id=1, source_target_pairs={{0,4},{4,8},{8,12},{12,16},{16,20},{20,24},{24,28},{28,32},{32,36}... | collective-permute-start | bytes 1572872 | tf_op jit(solution)/shard_map/ppermute | solution.py:12
  142.1 8.5 %collective-permute-start.3 = (bf16[512,512]{1,0:T(8,128)(2,1)S(1)}, bf16[512,512]{1,0:T(8,128)(2,1)S(1)}, u32[]{:S(2)}, u32[]{:S(2)}) collective-permute-start(bf16[512,512]{1,0:T(8,128)(2,1)S(1)} %bitcast.53), channel_id=1, source_target_pairs={{4,0},{8,4},{12,8},{16,12},{20,16},{24,20},{28,24},{32,28},{36,32}... | collective-permute-start | bytes 1572872 | tf_op jit(solution)/shard_map/ppermute | solution.py:12
  149.5 3.7 copy-start.8
  153.1 85.9 %copy-start.5 = (bf16[512,512]{1,0:T(8,128)(2,1)S(1)}, bf16[512,512]{1,0:T(8,128)(2,1)}, u32[]{:S(2)}) copy-start(bf16[512,512]{1,0:T(8,128)(2,1)} %param.18) | copy-start | bytes 1572868
  153.1 322.6 %all-reduce.3.cloned.1.call-start = ((), (), s32[]{:S(2)}) async-start(), calls=%async_computation.5 | async-start | bytes 4194304 | tf_op jit(solution)/shard_map/psum | solution.py:78
Sparse Core Ops, SparseCore 0:
  62.7 29.6 all-gather.1
  153.2 52.8 reduce-scatter.1
  213.1 262.4 all-reduce.2
where the time goes:
time: 487 us
  waiting for transfers between devices  288 us (59%)
  blocking collectives  83 us (17%)
  local copies, waits for them, and re-layouts  31.1 us (6%)
  starting transfers between devices  31.1 us (6%)
  matrix products  25.2 us (5%)
  other arithmetic  14.6 us (3%)
  between operations  14.1 us (3%)
    psum x1, waiting for transfers between devices, shards(): lax.psum((contract_rows(features, dz), contract_rows(agg, dz), jnp.sum(dz...  234 us
    psum x1, blocking collectives, shards(): lax.psum((contract_rows(features, dz), contract_rows(agg, dz), jnp.sum(dz...  83 us
    all_gather x1, waiting for transfers between devices, shards(): whole = lax.all_gather(features, 'rep', axis=0, tiled=True)  29.2 us
    all_to_all x1, waiting for transfers between devices, shards(): lax.all_to_all(x_loader[order], 'dom', split_axis=0, concat_axis=0, tiled...  15.8 us
    dot_general x1, matrix products, shards(): jnp.einsum('en,nbf->ebf', selector, terms.reshape(-1, 128, width), precis...  12.3 us
    all_to_all x1, starting transfers between devices, shards(): lax.all_to_all((owner_index % rows)[order], 'dom', split_axis=0, concat_a...  12.1 us
    ppermute x2, starting transfers between devices, shifted(): lax.ppermute(value, axis, [(source, source + steps) for source in range(f...  10.4 us
  transfers between devices with their start and end apart: 9, of which 5 were waited for; matrix products, arithmetic and copies ran while one was open for 4% of the time, Pallas kernels for 0%

commit v1 on v0

--- a/solution.py
+++ b/solution.py
@@ -62,7 +62,9 @@
     local_cols = tile_cols - first_tile
     masked = tile_vals * tile_live.astype(jnp.bfloat16)[:, :, None, None]
     degree = 1.0 + jnp.sum(masked, axis=(1, 3), dtype=jnp.float32)
-    whole = lax.all_gather(features, "rep", axis=0, tiled=True)
+    whole = jnp.concatenate(
+        lax.all_to_all(jnp.stack([features] * lax.axis_size("rep")), "rep", 0, 0), axis=0
+    )
     extended = with_halo(whole, (("dom", 0),), rim_rows)
     picked = extended.reshape(-1, 128, width)[local_cols]
     summed = jnp.einsum("tkab,tkbf->taf", masked, picked, preferred_element_type=jnp.float32)

time: 487 us -> 453 us (0.930)
  waiting for transfers between devices: 288 us -> 245 us
    psum x1, waiting for transfers between devices: 234 us -> 199 us  [shards(): lax.psum((contract_rows(features, dz), contract_rows(agg, dz), jnp.sum(dz...]
    all_gather x1 -> x0, waiting for transfers between devices: 29.2 us -> none  [shards(): whole = lax.all_gather(features, 'rep', axis=0, tiled=True)]
    all_to_all x0 -> x1, waiting for transfers between devices: none -> 23.2 us  [shards(): lax.all_to_all(jnp.stack([features] * lax.axis_size('rep')), 'rep', 0, 0)]
  transfers between devices with their start and end apart: 9 -> 9, of which waited for: 5 -> 5; matrix products, arithmetic and copies ran while one was open for 4% -> 5% of each run, Pallas kernels for 0% -> 0%
where the time goes in v1:
time: 453 us
  waiting for transfers between devices  245 us (54%)
  blocking collectives  83.4 us (18%)
  starting transfers between devices  35.3 us (8%)
  local copies, waits for them, and re-layouts  30.8 us (7%)
  matrix products  26.2 us (6%)
  between operations  15.8 us (3%)
  other arithmetic  15.7 us (3%)
    psum x1, waiting for transfers between devices, shards(): lax.psum((contract_rows(features, dz), contract_rows(agg, dz), jnp.sum(dz...  199 us
    psum x1, blocking collectives, shards(): lax.psum((contract_rows(features, dz), contract_rows(agg, dz), jnp.sum(dz...  83.4 us
    all_to_all x1, waiting for transfers between devices, shards(): lax.all_to_all(jnp.stack([features] * lax.axis_size('rep')), 'rep', 0, 0)  23.2 us
    all_to_all x1, waiting for transfers between devices, shards(): lax.all_to_all(x_loader[order], 'dom', split_axis=0, concat_axis=0, tiled...  15.8 us
    dot_general x1, matrix products, shards(): jnp.einsum('en,nbf->ebf', selector, terms.reshape(-1, 128, width), precis...  12.3 us
    all_to_all x1, starting transfers between devices, shards(): lax.all_to_all((owner_index % rows)[order], 'dom', split_axis=0, concat_a...  12.1 us
    ppermute x2, starting transfers between devices, shifted(): lax.ppermute(value, axis, [(source, source + steps) for source in range(f...  10.4 us
  transfers between devices with their start and end apart: 9, of which 5 were waited for; matrix products, arithmetic and copies ran while one was open for 5% of the time, Pallas kernels for 0%

profile of v1, /device:TPU:2, one launch (start us, length us, event | category | flops | bytes accessed | tf_op | source)
XLA Modules:
  0.0 452.7 jit_solution(10412210641896423649)
XLA Ops:
  8.8 3.8 sort.17
  12.6 3.5 gather_fusion
  16.8 12.1 %all-to-all-start = ((s32[64,8,1]{1,2,0:T(1,128)}), s32[64,8,1]{1,2,0:T(1,128)S(1)}, u32[]{:S(2)}, u32[]{:S(2)}) async-start(s32[64,8,1]{1,2,0:T(1,128)} %bitcast), calls=%async_computation | async-start | bytes 65536 | tf_op jit(solution)/shard_map/all_to_all | solution.py:58
  28.9 2.6 gather_fusion.1
  31.5 6.8 %all-to-all-done = s32[64,8,1]{1,2,0:T(1,128)S(1)} async-done(((s32[64,8,1]{1,2,0:T(1,128)}), s32[64,8,1]{1,2,0:T(1,128)S(1)}, u32[]{:S(2)}, u32[]{:S(2)}) %all-to-all-start) | async-done | bytes 2080 | tf_op jit(solution)/shard_map/all_to_all | solution.py:58
  38.3 4.6 %all-to-all-start.1 = ((bf16[64,8,512]{2,1,0:T(8,128)(2,1)}), bf16[64,8,512]{2,1,0:T(8,128)(2,1)S(1)}, u32[]{:S(2)}, u32[]{:S(2)}) async-start(bf16[64,8,512]{2,1,0:T(8,128)(2,1)} %bitcast.2), calls=%async_computation.1 | async-start | bytes 1048576 | tf_op jit(solution)/shard_map/all_to_all | solution.py:57
  44.3 15.8 %all-to-all-done.1 = bf16[64,8,512]{2,1,0:T(8,128)(2,1)S(1)} async-done(((bf16[64,8,512]{2,1,0:T(8,128)(2,1)}), bf16[64,8,512]{2,1,0:T(8,128)(2,1)S(1)}, u32[]{:S(2)}, u32[]{:S(2)}) %all-to-all-start.1) | async-done | bytes 524320 | tf_op jit(solution)/shard_map/all_to_all | solution.py:57
  60.2 2.5 scatter_custom_fusion
  64.2 4.8 %all-to-all-start.2 = ((bf16[4,512,512]{2,1,0:T(8,128)(2,1)}), bf16[4,512,512]{2,1,0:T(8,128)(2,1)S(1)}, u32[]{:S(2)}, u32[]{:S(2)}) async-start(bf16[4,512,512]{2,1,0:T(8,128)(2,1)} %stack.2), calls=%async_computation.2 | async-start | bytes 4194304 | tf_op jit(solution)/shard_map/all_to_all | solution.py:66
  71.0 23.2 %all-to-all-done.2 = bf16[4,512,512]{2,1,0:T(8,128)(2,1)S(1)} async-done(((bf16[4,512,512]{2,1,0:T(8,128)(2,1)}), bf16[4,512,512]{2,1,0:T(8,128)(2,1)S(1)}, u32[]{:S(2)}, u32[]{:S(2)}) %all-to-all-start.2) | async-done | bytes 2097184 | tf_op jit(solution)/shard_map/all_to_all | solution.py:66
  95.2 2.1 collective-permute-start
  98.7 2.4 fusion.27
  102.1 2.8 pad_maximum_fusion
  104.9 7.0 %gather_fusion.2 = bf16[48,128,512]{2,1,0:T(8,128)(2,1)} fusion(bf16[24,128,512]{2,1,0:T(8,128)(2,1)} %bitcast.55, s32[1024]{0:T(1024)S(1)} %pad_clamp_fusion), kind=kCustom, calls=%fused_computation.2 | custom fusion | bytes 12583104 | tf_op jit(solution)/shard_map/gather | solution.py:69
  111.9 4.0 fusion.5
  120.1 12.3 %fusion.26 = (bf16[24,128,512]{2,0,1:T(8,128)(2,1)S(1)}, f32[24,128,512]{2,0,1:T(8,128)S(1)}) fusion(f32[48,128,512]{2,1,0:T(8,128)S(1)} %bitcast.54, s32[48]{0:T(128)S(1)} %eq.17), kind=kOutput, calls=%fused_computation.57 | convolution fusion | flops 907543680 | bytes 22020288 | tf_op jit(solution)/shard_map/en,nbf->ebf/dot_general | solution.py:99
  133.0 9.1 %collective-permute-start.2 = (bf16[512,512]{1,0:T(8,128)(2,1)S(1)}, bf16[512,512]{1,0:T(8,128)(2,1)S(1)}, u32[]{:S(2)}, u32[]{:S(2)}) collective-permute-start(bf16[512,512]{1,0:T(8,128)(2,1)S(1)} %bitcast.60), channel_id=1, source_target_pairs={{0,4},{4,8},{8,12},{12,16},{16,20},{20,24},{24,28},{28,32},{32,36}... | collective-permute-start | bytes 1572872 | tf_op jit(solution)/shard_map/ppermute | solution.py:12
  144.8 4.4 copy.29
  150.7 2.4 fusion.12
  156.0 83.4 %psum.23 = f32[512]{0:T(512)} all-reduce(f32[512]{0:T(512)S(1)} %get-tuple-element.33), channel_id=1, replica_groups=mesh['dom'=64,'rep'=4] {'dom','rep'}, use_global_device_ids=true, to_apply=%region_7.8 | all-reduce | flops 512 | bytes 4096 | tf_op jit(solution)/shard_map/psum | solution.py:80
  239.9 2.2 add_convert_fusion
  242.1 198.6 %all-reduce.3.cloned.1.call-done = (f32[512,512]{1,0:T(8,128)}, f32[512,512]{1,0:T(8,128)}) async-done(((f32[512,512]{1,0:T(8,128)}, f32[512,512]{1,0:T(8,128)}), (f32[512,512]{1,0:T(8,128)}, f32[512,512]{1,0:T(8,128)})) %all-reduce.3.cloned.1.call-update) | async-done | bytes 2097168 | tf_op jit(solution)/shard_map/psum | solution.py:80
  440.7 2.3 copy.44
  443.0 2.3 copy.45
  (66 shorter events, 21.9 us)
Async XLA Ops:
  8.0 108.0 %copy-start = (bf16[512,512]{1,0:T(8,128)(2,1)S(1)}, bf16[512,512]{1,0:T(8,128)(2,1)}, u32[]{:S(2)}) copy-start(bf16[512,512]{1,0:T(8,128)(2,1)} %param.19) | copy-start | bytes 1572868
  8.0 20.9 %copy-start.2 = (bf16[512,512]{1,0:T(8,128)(2,1)S(1)}, bf16[512,512]{1,0:T(8,128)(2,1)}, u32[]{:S(2)}) copy-start(bf16[512,512]{1,0:T(8,128)(2,1)} %param.13) | copy-start | bytes 1572868
  16.8 21.5 %all-to-all-start = ((s32[64,8,1]{1,2,0:T(1,128)}), s32[64,8,1]{1,2,0:T(1,128)S(1)}, u32[]{:S(2)}, u32[]{:S(2)}) async-start(s32[64,8,1]{1,2,0:T(1,128)} %bitcast), calls=%async_computation | async-start | bytes 65536 | tf_op jit(solution)/shard_map/all_to_all | solution.py:58
  38.3 21.8 %all-to-all-start.1 = ((bf16[64,8,512]{2,1,0:T(8,128)(2,1)}), bf16[64,8,512]{2,1,0:T(8,128)(2,1)S(1)}, u32[]{:S(2)}, u32[]{:S(2)}) async-start(bf16[64,8,512]{2,1,0:T(8,128)(2,1)} %bitcast.2), calls=%async_computation.1 | async-start | bytes 1048576 | tf_op jit(solution)/shard_map/all_to_all | solution.py:57
  43.0 26.1 %copy-start.9 = (s32[4,12]{1,0:T(4,128)S(1)}, s32[4,12]{1,0:T(4,128)}, u32[]{:S(2)}) copy-start(s32[4,12]{1,0:T(4,128)} %param.16) | copy-start | bytes 580
  43.0 26.1 %copy-start.8 = (s32[4,12]{1,0:T(4,128)S(1)}, s32[4,12]{1,0:T(4,128)}, u32[]{:S(2)}) copy-start(s32[4,12]{1,0:T(4,128)} %param.17) | copy-start | bytes 580
  64.2 30.0 %all-to-all-start.2 = ((bf16[4,512,512]{2,1,0:T(8,128)(2,1)}), bf16[4,512,512]{2,1,0:T(8,128)(2,1)S(1)}, u32[]{:S(2)}, u32[]{:S(2)}) async-start(bf16[4,512,512]{2,1,0:T(8,128)(2,1)} %stack.2), calls=%async_computation.2 | async-start | bytes 4194304 | tf_op jit(solution)/shard_map/all_to_all | solution.py:66
  69.0 170.9 %reduce-scatter.2.cloned.1.call-start = ((), (), s32[]{:S(2)}) async-start(), calls=%async_computation.4 | async-start | bytes 5242880 | tf_op jit(solution)/shard_map/reduce_scatter | solution.py:108
  95.2 5.9 %collective-permute-start = (bf16[512,512]{1,0:T(8,128)(2,1)}, bf16[512,512]{1,0:T(8,128)(2,1)}, u32[]{:S(2)}, u32[]{:S(2)}) collective-permute-start(bf16[512,512]{1,0:T(8,128)(2,1)} %get-tuple-element.39), channel_id=1, source_target_pairs={{0,4},{4,8},{8,12},{12,16},{16,20},{20,24},{24,28},{28,32},{32,36}... | collective-permute-start | bytes 1572872 | tf_op jit(solution)/shard_map/ppermute | solution.py:20
  97.3 4.8 %collective-permute-start.1 = (bf16[512,512]{1,0:T(8,128)(2,1)}, bf16[512,512]{1,0:T(8,128)(2,1)}, u32[]{:S(2)}, u32[]{:S(2)}) collective-permute-start(bf16[512,512]{1,0:T(8,128)(2,1)} %get-tuple-element.40), channel_id=1, source_target_pairs={{4,0},{8,4},{12,8},{16,12},{20,16},{24,20},{28,24},{32,28},{36,32}... | collective-permute-start | bytes 1572872 | tf_op jit(solution)/shard_map/ppermute | solution.py:23
  104.9 7.0 %copy-start.3 = (bf16[4,12,128,128]{3,2,1,0:T(8,128)(2,1)S(1)}, bf16[4,12,128,128]{3,2,1,0:T(8,128)(2,1)}, u32[]{:S(2)}) copy-start(bf16[4,12,128,128]{3,2,1,0:T(8,128)(2,1)} %param.15) | copy-start | bytes 4718596
  111.9 4.1 copy-start.5
  111.9 4.1 copy-start.10
  111.9 4.1 copy-start.11
  115.9 2.3 copy-start.6
  133.0 16.5 %collective-permute-start.2 = (bf16[512,512]{1,0:T(8,128)(2,1)S(1)}, bf16[512,512]{1,0:T(8,128)(2,1)S(1)}, u32[]{:S(2)}, u32[]{:S(2)}) collective-permute-start(bf16[512,512]{1,0:T(8,128)(2,1)S(1)} %bitcast.60), channel_id=1, source_target_pairs={{0,4},{4,8},{8,12},{12,16},{16,20},{20,24},{24,28},{28,32},{32,36}... | collective-permute-start | bytes 1572872 | tf_op jit(solution)/shard_map/ppermute | solution.py:12
  142.2 8.5 %collective-permute-start.3 = (bf16[512,512]{1,0:T(8,128)(2,1)S(1)}, bf16[512,512]{1,0:T(8,128)(2,1)S(1)}, u32[]{:S(2)}, u32[]{:S(2)}) collective-permute-start(bf16[512,512]{1,0:T(8,128)(2,1)S(1)} %bitcast.59), channel_id=1, source_target_pairs={{4,0},{8,4},{12,8},{16,12},{20,16},{24,20},{28,24},{32,28},{36,32}... | collective-permute-start | bytes 1572872 | tf_op jit(solution)/shard_map/ppermute | solution.py:12
  149.5 3.6 copy-start.7
  153.1 86.4 %copy-start.4 = (bf16[512,512]{1,0:T(8,128)(2,1)S(1)}, bf16[512,512]{1,0:T(8,128)(2,1)}, u32[]{:S(2)}) copy-start(bf16[512,512]{1,0:T(8,128)(2,1)} %param.18) | copy-start | bytes 1572868
  153.1 287.6 %all-reduce.3.cloned.1.call-start = ((), (), s32[]{:S(2)}) async-start(), calls=%async_computation.5 | async-start | bytes 4194304 | tf_op jit(solution)/shard_map/psum | solution.py:80
  156.0 289.2 %copy-start.1 = (bf16[512,512]{1,0:T(8,128)(2,1)S(1)}, bf16[512,512]{1,0:T(8,128)(2,1)}, u32[]{:S(2)}) copy-start(bf16[512,512]{1,0:T(8,128)(2,1)} %param.19) | copy-start | bytes 1572868
Sparse Core Ops, SparseCore 0:
  153.2 52.8 reduce-scatter.1
Sparse Core Ops, SparseCore 1:
  160.6 280.1 all-reduce.2
